TPU v7x, 512 devices: a whole 4x8x8 slice. The times are simulated.
512 devices in a mesh: lon: 128 (over z, x, y_hi, core), lat: 4 (over y_lo).
Axes of the slice: x: 4, y: 8 (y_hi: 2, y_lo: 4; y = y_hi * 4 + y_lo), z: 8, core: 2. Of those that a mesh axis runs over, the one named last changes fastest.
Arguments:
- state: float32 [2, 4, 5760, 512], P(None, None, 'lon', 'lat'), may hold values from -6 to 6
- courant: float32 [2, 5760, 512], P(None, 'lon', 'lat'), may hold values from 1 to 34560
- band_mask: int32 [512], P('lat'), may hold values 0 or 1
Outputs:
- updated: float32 [2, 4, 5760, 512], P(None, None, 'lon', 'lat')
All inputs are finite; a program needn't handle non-finite values. No bound on the sum of `band_mask` on one device may be relied on, other than what follows from the above.
Results may differ from a plain program's by a relative error of at most 0.00029.
Values sent between devices are 32-bit elements; how exact they have to be, the bound alone decides.
No kernel may reach another device: no remote copies, remote signals or barrier semaphores. Data moves between devices by JAX's collectives and lax.ppermute only.
A program may use at most 64 MiB of HBM per device.

v0:
```python
import jax
import jax.numpy as jnp
from jax import lax
from jax.sharding import PartitionSpec as P

ITERS = 2


def padded_2(block, sides, width):
    for axis, dim in sides:
        count = lax.axis_size(axis)
        forward = [(i, i + 1) for i in range(count - 1)]
        forward.append((count - 1, 0))
        backward = [(target, source) for source, target in forward]
        low = lax.ppermute(
            lax.slice_in_dim(block, block.shape[dim] - width, None, axis=dim), axis, forward
        )
        high = lax.ppermute(lax.slice_in_dim(block, 0, width, axis=dim), axis, backward)
        block = jnp.concatenate([low, block, high], axis=dim)
    return block


def from_behind(value, axis, steps):
    count = lax.axis_size(axis)
    pairs = [(source, (source + steps) % count) for source in range(count)]
    return lax.ppermute(value, axis, pairs)


def carried_in(part, axis, combine, identity):
    place = lax.axis_index(axis)
    gathered = jax.tree.map(lambda a: lax.all_gather(a, axis), part)
    state = jax.tree.map(lambda a, e: jnp.zeros_like(a) + jnp.asarray(e, a.dtype), part, identity)

    def one(lap, state):
        return combine(
            state, jax.tree.map(lambda a: lax.dynamic_index_in_dim(a, lap, 0, False), gathered)
        )

    return lax.fori_loop(0, place, one, state)


def broadcast(value, axis, source):
    kept = jnp.where(lax.axis_index(axis) == source, value, 0).astype(value.dtype)
    return lax.psum(kept, axis)


def compose(earlier, later):
    return (later[0] * earlier[0], later[0][..., None, :] * earlier[1] + later[1])


def local_level(operands):
    logs_level, weights_level = operands
    spread_log = logs_level[:, None, :] - logs_level[None, :, :]
    count = logs_level.shape[0]
    below_diag = (jnp.arange(count)[:, None] >= jnp.arange(count)[None, :])[:, :, None]
    green = jnp.where(below_diag, jnp.exp(jnp.minimum(spread_log, 0.0)), 0.0)
    return jnp.einsum("ikr,fkr->fir", green, weights_level, precision=lax.Precision.HIGHEST)


def tendency(field, turning, first_band, last_band, half_cycle):
    padded = padded_2(field, (("lon", 2), ("lat", 3)), 1)
    poles = jnp.stack((field[..., 0], field[..., -1]), 0)
    across = from_behind(poles, "lon", half_cycle)
    flips = jnp.array([-1.0, -1.0, 1.0, 1.0], jnp.float32)[None, :, None]
    north_rim = jnp.where(first_band, across[0] * flips, padded[:, :, 1:-1, 0])
    south_rim = jnp.where(last_band, across[1] * flips, padded[:, :, 1:-1, -1])
    padded = padded.at[:, :, 1:-1, 0].set(north_rim).at[:, :, 1:-1, -1].set(south_rim)
    north_rows = padded[:, :, 1:-1, :-2]
    south_rows = padded[:, :, 1:-1, 2:]
    east_cells = padded[:, :, 2:, 1:-1]
    west_cells = padded[:, :, :-2, 1:-1]
    u_wind = field[:, 0:1]
    v_wind = field[:, 1:2]
    result = 0.1 * (east_cells + west_cells - 2.0 * field) + 0.1 * (
        north_rows + south_rows - 2.0 * field
    )
    result = result - 0.25 * v_wind * (north_rows - south_rows)
    coriolis = jnp.concatenate(
        [turning * v_wind, -turning * u_wind, jnp.zeros_like(field[:, 2:])], axis=1
    )
    return result + coriolis


def local(state, courant, band_mask):
    rows = state.shape[3]
    lat_index = lax.axis_index("lat")
    lat_count = lax.axis_size("lat")
    half_cycle = lax.axis_size("lon") // 2
    total_rows = rows * lat_count
    row_ids = lat_index * rows + jnp.arange(rows, dtype=jnp.int32)
    latitude = jnp.pi / 2 - (row_ids.astype(jnp.float32) + 0.5) * jnp.pi / total_rows
    turning = 0.5 * jnp.sin(latitude)
    first_band = lat_index == 0
    last_band = lat_index == lat_count - 1
    inverse = 1.0 / (1.0 + courant)
    logs = jnp.cumsum(-jnp.log1p(1.0 / courant), axis=1)
    carried = jnp.exp(logs)
    map_gain = carried[:, -1, :]
    in_band = (band_mask == 1)[None, None, None, :]
    estimate = state
    for sweep in range(ITERS):
        middle = 0.5 * (state + estimate)
        star = state + tendency(middle, turning, first_band, last_band, half_cycle)
        partial_value = lax.map(local_level, (logs, star * inverse[:, None]))
        ends = partial_value[:, :, -1, :]
        identity = (jnp.ones_like(map_gain), jnp.zeros_like(ends))
        prior_a, prior_b = carried_in((map_gain, ends), "lon", compose, identity)
        whole = compose((prior_a, prior_b), (map_gain, ends))
        total_a, total_b = (
            broadcast(whole[0], "lon", lax.axis_size("lon") - 1),
            broadcast(whole[1], "lon", lax.axis_size("lon") - 1),
        )
        wrapped = total_b / (1.0 - total_a)[:, None, :]
        inflow = prior_b + prior_a[:, None, :] * wrapped
        solved = partial_value + carried[:, None] * inflow[:, :, None, :]
        estimate = jnp.where(in_band, solved, star)
    return estimate


def solution(mesh):
    in_specs = (P(None, None, "lon", "lat"), P(None, "lon", "lat"), P("lat"))
    out_specs = P(None, None, "lon", "lat")
    return jax.shard_map(local, mesh=mesh, in_specs=in_specs, out_specs=out_specs, check_vma=False)
```

profile of v0, /device:TPU:24, one launch (start us, length us, event | category | flops | bytes accessed | tf_op | source)
XLA Modules:
  0.0 1620.4 jit_solution(11507833808939434225)
XLA Ops:
  3.0 15.3 collective-permute-start.1
  18.8 7.5 collective-permute-start.4
  26.7 214.2 %all-gather = f32[256,1,128]{2,1,0:T(1,128)S(1)} all-gather(f32[2,1,128]{2,1,0:T(1,128)S(1)} %slice.276), channel_id=2, replica_groups=mesh['lon'=128,'lat'=4] {'lon'}, dimensions={0}, use_global_device_ids=true | all-gather | bytes 132096 | tf_op jit(solution)/shard_map/all_gather | solution.py:31
  241.5 4.8 collective-permute-start.2
  248.8 2.7 collective-permute-done.2
  251.5 5.3 collective-permute-done.3
  257.8 2.8 scatter.14
  260.6 14.9 scatter.15
  276.3 11.2 while.48
  276.6 5.3 fusion.69
  282.2 5.3 fusion.69
  287.9 218.6 %all-gather.1 = f32[256,4,1,128]{3,1,2,0:T(4,128)S(1)} all-gather(f32[2,4,1,128]{3,1,2,0:T(4,128)S(1)} %slice.277), channel_id=3, replica_groups=mesh['lon'=128,'lat'=4] {'lon'}, dimensions={0}, use_global_device_ids=true | all-gather | bytes 528384 | tf_op jit(solution)/shard_map/all_gather | solution.py:31
  506.5 415.3 %all-reduce.1 = (f32[2,4,128]{2,1,0:T(4,128)S(1)}, f32[2,128]{1,0:T(2,128)S(1)}) all-reduce(f32[2,4,128]{2,1,0:T(4,128)S(1)} %fusion.47, f32[2,128]{1,0:T(2,128)S(1)} %multiply_select_fusion.1), channel_id=1, replica_groups=mesh['lon'=128,'lat'=4] {'lon'}, use_global_device_ids=true, to_apply=%region_5.6 | all-reduce | flops 1280 | bytes 10240 | tf_op jit(solution)/shard_map/psum | solution.py:44
  924.6 11.8 collective-permute-start.6
  936.3 4.1 collective-permute-start.9
  940.8 4.4 collective-permute-start.7
  948.4 6.2 collective-permute-done.8
  955.5 2.8 scatter.16
  958.3 14.9 scatter.19
  974.0 11.2 while.50
  974.3 5.3 fusion.73
  979.9 5.3 fusion.73
  985.7 215.4 %all-gather.2 = f32[256,4,1,128]{3,1,2,0:T(4,128)S(1)} all-gather(f32[2,4,1,128]{3,1,2,0:T(4,128)S(1)} %slice_bitcast_fusion.4), channel_id=4, replica_groups=mesh['lon'=128,'lat'=4] {'lon'}, dimensions={0}, use_global_device_ids=true | all-gather | bytes 528384 | tf_op jit(solution)/shard_map/all_gather | solution.py:31
  1201.1 418.4 %all-reduce = (f32[2,4,128]{2,1,0:T(4,128)S(1)}, f32[2,128]{1,0:T(2,128)S(1)}) all-reduce(f32[2,4,128]{2,1,0:T(4,128)S(1)} %fusion.46, f32[2,128]{1,0:T(2,128)S(1)} %multiply_select_fusion), channel_id=1, replica_groups=mesh['lon'=128,'lat'=4] {'lon'}, use_global_device_ids=true, to_apply=%region_11.12 | all-reduce | flops 1280 | bytes 10240 | tf_op jit(solution)/shard_map/psum | solution.py:44
  (102 shorter events, 19.2 us)
Async XLA Ops:
  1.0 240.1 %collective-permute-start = (f32[2,4,1,128]{3,0,2,1:T(2,128)S(1)}, f32[2,4,1,128]{3,0,2,1:T(2,128)S(1)}, u32[]{:S(2)}, u32[]{:S(2)}) collective-permute-start(f32[2,4,1,128]{3,0,2,1:T(2,128)S(1)} %get-tuple-element.316), channel_id=1, source_target_pairs={{0,4},{4,8},{8,12},{12,16},{16,20},{20,24},{24,28},{28,32},{32,36}... | collective-permute-start | bytes 12296 | tf_op jit(solution)/shard_map/ppermute | solution.py:15
  3.0 23.5 %copy-start.1 = (f32[2,45,128]{2,0,1:T(2,128)S(1)}, f32[2,45,128]{2,0,1:T(2,128)}, u32[]{:S(2)}) copy-start(f32[2,45,128]{2,0,1:T(2,128)} %param.22) | copy-start | bytes 138244
  3.0 238.2 %collective-permute-start.1 = (f32[2,4,1,128]{3,0,2,1:T(2,128)S(1)}, f32[2,4,1,128]{3,0,2,1:T(2,128)S(1)}, u32[]{:S(2)}, u32[]{:S(2)}) collective-permute-start(f32[2,4,1,128]{3,0,2,1:T(2,128)S(1)} %get-tuple-element.317), channel_id=1, source_target_pairs={{4,0},{8,4},{12,8},{16,12},{20,16},{24,20},{28,24},{32,28},{36,32}... | collective-permute-start | bytes 12296 | tf_op jit(solution)/shard_map/ppermute | solution.py:18
  18.5 8.1 copy-start.3
  18.8 229.7 %collective-permute-start.4 = (f32[2,2,4,45]{3,2,1,0:T(4,128)S(1)}, f32[2,2,4,45]{3,2,1,0:T(4,128)S(1)}, u32[]{:S(2)}, u32[]{:S(2)}) collective-permute-start(f32[2,2,4,45]{3,2,1,0:T(4,128)S(1)} %pad_maximum_fusion.4), channel_id=1, source_target_pairs={{0,256},{4,260},{8,264},{12,268},{16,272},{20,276},{24,280},{28,28... | collective-permute-start | bytes 8648 | tf_op jit(solution)/shard_map/ppermute | solution.py:26
  241.5 10.0 collective-permute-start.2
  246.4 10.5 collective-permute-start.3
  248.8 8.7 copy-start.2
  257.8 17.8 %copy-start = (f32[2,4,45,128]{3,1,2,0:T(4,128)S(1)}, f32[2,4,45,128]{3,1,2,0:T(4,128)}, u32[]{:S(2)}) copy-start(f32[2,4,45,128]{3,1,2,0:T(4,128)} %param.21) | copy-start | bytes 552964
  922.6 17.8 %collective-permute-start.5 = (f32[2,4,1,128]{3,0,2,1:T(2,128)S(1)}, f32[2,4,1,128]{3,0,2,1:T(2,128)S(1)}, u32[]{:S(2)}, u32[]{:S(2)}) collective-permute-start(f32[2,4,1,128]{3,0,2,1:T(2,128)S(1)} %get-tuple-element.309), channel_id=1, source_target_pairs={{0,4},{4,8},{8,12},{12,16},{16,20},{20,24},{24,28},{28,32},{32,36}... | collective-permute-start | bytes 12296 | tf_op jit(solution)/shard_map/ppermute | solution.py:15
  924.6 15.9 collective-permute-start.6
  936.3 10.8 collective-permute-start.9
  940.8 7.6 collective-permute-start.7
  945.2 9.3 collective-permute-start.8
where the time goes:
time: 1620 us
  blocking collectives  1480 us (91%)
  starting transfers between devices  55.8 us (3%)
  local copies, waits for them, and re-layouts  40.8 us (3%)
  matrix products  21.1 us (1%)
    psum x2, blocking collectives, broadcast(): return lax.psum(kept, axis)  834 us
    all_gather x3, blocking collectives, carried_in(): gathered = jax.tree.map(lambda a: lax.all_gather(a, axis), part)  648 us
    scatter x4, local copies, waits for them, and re-layouts, tendency(): padded.at[:, :, 1:-1, 0].set(north_rim).at[:, :, 1:-1, -1].set(south_rim)  35.5 us
  transfers between devices with their start and end apart: 10, of which 4 were waited for; matrix products, arithmetic and copies ran while one was open for 0% of the time, Pallas kernels for 0%

commit v1 on v0

--- a/solution.py
+++ b/solution.py
@@ -41,7 +41,7 @@
 
 def broadcast(value, axis, source):
     kept = jnp.where(lax.axis_index(axis) == source, value, 0).astype(value.dtype)
-    return lax.psum(kept, axis)
+    return jnp.sum(lax.all_gather(kept, axis), axis=0)
 
 
 def compose(earlier, later):

time: 1620 us -> 1670 us (1.031)
  the two profiles are of different devices: /device:TPU:24 before, /device:TPU:1 now
where the time goes in v1:
time: 1670 us
  blocking collectives  1540 us (92%)
  starting transfers between devices  48.9 us (3%)
  local copies, waits for them, and re-layouts  40.8 us (2%)
  matrix products  21.1 us (1%)
    all_gather x4, blocking collectives, broadcast(): return jnp.sum(lax.all_gather(kept, axis), axis=0)  883 us
    all_gather x3, blocking collectives, carried_in(): gathered = jax.tree.map(lambda a: lax.all_gather(a, axis), part)  657 us
    scatter x4, local copies, waits for them, and re-layouts, tendency(): padded.at[:, :, 1:-1, 0].set(north_rim).at[:, :, 1:-1, -1].set(south_rim)  35.5 us
  transfers between devices with their start and end apart: 10, of which 5 were waited for; matrix products, arithmetic and copies ran while one was open for 0% of the time, Pallas kernels for 0%

profile of v1, /device:TPU:1, one launch (start us, length us, event | category | flops | bytes accessed | tf_op | source)
XLA Modules:
  0.0 1673.5 jit_solution(9804965991067944642)
XLA Ops:
  1.0 8.8 collective-permute-start
  12.5 10.6 collective-permute-start.4
  23.5 221.4 %all-gather = f32[256,1,128]{2,1,0:T(1,128)S(1)} all-gather(f32[2,1,128]{2,1,0:T(1,128)S(1)} %slice.276), channel_id=2, replica_groups=mesh['lon'=128,'lat'=4] {'lon'}, dimensions={0}, use_global_device_ids=true | all-gather | bytes 132096 | tf_op jit(solution)/shard_map/all_gather | solution.py:31
  247.9 5.0 collective-permute-start.3
  255.5 4.6 collective-permute-done.3
  263.9 14.9 scatter.15
  279.6 11.2 while.48
  279.9 5.3 fusion.69
  285.4 5.3 fusion.69
  291.2 218.4 %all-gather.1 = f32[256,4,1,128]{3,1,2,0:T(4,128)S(1)} all-gather(f32[2,4,1,128]{3,1,2,0:T(4,128)S(1)} %slice.277), channel_id=3, replica_groups=mesh['lon'=128,'lat'=4] {'lon'}, dimensions={0}, use_global_device_ids=true | all-gather | bytes 528384 | tf_op jit(solution)/shard_map/all_gather | solution.py:31
  509.7 226.6 %all-gather.2 = f32[256,4,128]{2,1,0:T(4,128)S(1)} all-gather(f32[2,4,128]{2,1,0:T(4,128)S(1)} %fusion.47), channel_id=4, replica_groups=mesh['lon'=128,'lat'=4] {'lon'}, dimensions={0}, use_global_device_ids=true | all-gather | bytes 528384 | tf_op jit(solution)/shard_map/all_gather | solution.py:44
  736.2 213.9 %all-gather.7 = f32[128,2,128]{2,1,0:T(2,128)S(1)} all-gather(f32[1,2,128]{2,1,0:T(2,128)S(1)} %select_bitcast_fusion.1), channel_id=5, replica_groups=mesh['lon'=128,'lat'=4] {'lon'}, dimensions={0}, use_global_device_ids=true | all-gather | bytes 132096 | tf_op jit(solution)/shard_map/all_gather | solution.py:44
  951.2 7.3 collective-permute-start.5
  960.4 3.8 collective-permute-start.9
  964.3 3.0 collective-permute-done.6
  969.9 4.9 collective-permute-start.8
  976.0 5.5 collective-permute-done.8
  985.3 14.9 scatter.19
  1001.0 11.2 while.50
  1001.3 5.3 fusion.73
  1006.9 5.3 fusion.73
  1012.7 217.5 %all-gather.4 = f32[256,4,1,128]{3,1,2,0:T(4,128)S(1)} all-gather(f32[2,4,1,128]{3,1,2,0:T(4,128)S(1)} %slice_bitcast_fusion.4), channel_id=6, replica_groups=mesh['lon'=128,'lat'=4] {'lon'}, dimensions={0}, use_global_device_ids=true | all-gather | bytes 528384 | tf_op jit(solution)/shard_map/all_gather | solution.py:31
  1230.2 228.2 %all-gather.5 = f32[256,4,128]{2,1,0:T(4,128)S(1)} all-gather(f32[2,4,128]{2,1,0:T(4,128)S(1)} %fusion.46), channel_id=7, replica_groups=mesh['lon'=128,'lat'=4] {'lon'}, dimensions={0}, use_global_device_ids=true | all-gather | bytes 528384 | tf_op jit(solution)/shard_map/all_gather | solution.py:44
  1458.4 213.9 %all-gather.8 = f32[128,2,128]{2,1,0:T(2,128)S(1)} all-gather(f32[1,2,128]{2,1,0:T(2,128)S(1)} %select_bitcast_fusion), channel_id=8, replica_groups=mesh['lon'=128,'lat'=4] {'lon'}, dimensions={0}, use_global_device_ids=true | all-gather | bytes 132096 | tf_op jit(solution)/shard_map/all_gather | solution.py:44
  (112 shorter events, 28.5 us)
Async XLA Ops:
  1.0 244.2 %collective-permute-start = (f32[2,4,1,128]{3,0,2,1:T(2,128)S(1)}, f32[2,4,1,128]{3,0,2,1:T(2,128)S(1)}, u32[]{:S(2)}, u32[]{:S(2)}) collective-permute-start(f32[2,4,1,128]{3,0,2,1:T(2,128)S(1)} %get-tuple-element.312), channel_id=1, source_target_pairs={{0,4},{4,8},{8,12},{12,16},{16,20},{20,24},{24,28},{28,32},{32,36}... | collective-permute-start | bytes 12296 | tf_op jit(solution)/shard_map/ppermute | solution.py:15
  9.9 13.3 copy-start.1
  9.9 235.3 %collective-permute-start.1 = (f32[2,4,1,128]{3,0,2,1:T(2,128)S(1)}, f32[2,4,1,128]{3,0,2,1:T(2,128)S(1)}, u32[]{:S(2)}, u32[]{:S(2)}) collective-permute-start(f32[2,4,1,128]{3,0,2,1:T(2,128)S(1)} %get-tuple-element.313), channel_id=1, source_target_pairs={{4,0},{8,4},{12,8},{16,12},{20,16},{24,20},{28,24},{32,28},{36,32}... | collective-permute-start | bytes 12296 | tf_op jit(solution)/shard_map/ppermute | solution.py:18
  12.2 11.2 copy-start.3
  12.5 240.3 %collective-permute-start.4 = (f32[2,2,4,45]{3,2,1,0:T(4,128)S(1)}, f32[2,2,4,45]{3,2,1,0:T(4,128)S(1)}, u32[]{:S(2)}, u32[]{:S(2)}) collective-permute-start(f32[2,2,4,45]{3,2,1,0:T(4,128)S(1)} %pad_maximum_fusion.4), channel_id=1, source_target_pairs={{0,256},{4,260},{8,264},{12,268},{16,272},{20,276},{24,280},{28,28... | collective-permute-start | bytes 8648 | tf_op jit(solution)/shard_map/ppermute | solution.py:26
  245.5 10.0 collective-permute-start.2
  247.9 12.2 collective-permute-start.3
  253.2 7.6 copy-start.2
  261.0 17.8 %copy-start = (f32[2,4,45,128]{3,1,2,0:T(4,128)S(1)}, f32[2,4,45,128]{3,1,2,0:T(4,128)}, u32[]{:S(2)}) copy-start(f32[2,4,45,128]{3,1,2,0:T(4,128)} %param.21) | copy-start | bytes 552964
  951.2 13.1 collective-permute-start.5
  958.5 8.8 collective-permute-start.6
  960.4 14.3 collective-permute-start.9
  967.7 8.3 collective-permute-start.7
  969.9 11.6 collective-permute-start.8
